TPU v7x, 512 devices: a whole 4x4x16 slice. The times are simulated.
512 devices in a mesh: rep: 32 (over z, core), row: 4 (over x), col: 4 (over y).
Axes of the slice: x: 4, y: 4, z: 16, core: 2. Of those that a mesh axis runs over, the one named last changes fastest.
Arguments:
- coordinates: bfloat16 [128, 32, 3, 128], P('rep')
- resample: int32 [32, 22], P('rep'), may hold values from 0 to 127, as said below
- block_slot: int32 [128], replicated, may hold values from 0 to 127, as said below
- lag_time: int32 [32], P('rep'), may hold values from 1 to 8
- atom_pairs: int32 [2, 4096], replicated, may hold values from 0 to 127, as said below
Outputs:
- instant_cov: bfloat16 [32, 4096, 4096], P('rep', 'row', 'col')
- lagged_cov: bfloat16 [32, 4096, 4096], P('rep', 'row', 'col')
Inputs may be any that keep to these rules, and one draw needn't show every extreme that they name: `resample`: the owner of a block is block_slot // 4. In each replicate at most 2 draws have one owner, and some owner has exactly 2; a block may be drawn more than once. `block_slot`: each slot holds exactly one block. `atom_pairs`: the two atoms of a feature differ, and no unordered pair of atoms appears twice.
All inputs are finite; a program needn't handle non-finite values.
Results may differ from a plain program's by a relative error of at most 0.0073.
Values may be sent and summed in bfloat16 or wider, within the bound.
No kernel may reach another device: no remote copies, remote signals or barrier semaphores. Data moves between devices by JAX's collectives and lax.ppermute only.
A program may use at most 64 MiB of HBM per device.

v0:
```python
import jax
import jax.numpy as jnp
from jax import lax
from jax.sharding import PartitionSpec as P

F = 4096
ATOMS = 128
BLOCK_LEN = 32
DRAWS = 22


def gather_blocks(coordinates, resample, block_slot):
    groups = lax.axis_size("row") * lax.axis_size("col")
    if BLOCK_LEN % groups:
        groups = 1
    frames = BLOCK_LEN // groups
    member = lax.axis_index("row") * lax.axis_size("col") + lax.axis_index("col")
    if groups == 1:
        member = 0
    piece = lax.dynamic_slice_in_dim(coordinates, member * frames, frames, axis=1)
    every = lax.all_gather(piece, "rep", axis=0, tiled=True)
    slots = jnp.take(block_slot, resample[0], axis=0)
    picked = jnp.take(every, slots, axis=0)
    if groups == 1:
        return picked
    return lax.all_gather(picked, ("row", "col"), axis=1, tiled=True)


def tile_features(chosen, atom_pairs, first_feature, width, shift):
    first_atoms = lax.dynamic_slice_in_dim(atom_pairs[0], first_feature, width)
    second_atoms = lax.dynamic_slice_in_dim(atom_pairs[1], first_feature, width)
    atom_ids = jnp.arange(chosen.shape[-1], dtype=jnp.int32)[:, None]
    signed = (
        (atom_ids == first_atoms[None, :]).astype(jnp.float32)
        - (atom_ids == second_atoms[None, :]).astype(jnp.float32)
    ).astype(jnp.bfloat16)
    flat = chosen.reshape(-1, chosen.shape[-1])
    difference = jnp.dot(flat, signed, preferred_element_type=jnp.float32).reshape(
        DRAWS, BLOCK_LEN, 3, width
    )
    squared = (
        difference[:, :, 0] * difference[:, :, 0]
        + difference[:, :, 1] * difference[:, :, 1]
        + difference[:, :, 2] * difference[:, :, 2]
    )
    features = jnp.sqrt(squared).astype(jnp.bfloat16)
    doubled = jnp.concatenate([features, features], axis=1)
    shifted = lax.dynamic_slice_in_dim(doubled, shift, BLOCK_LEN, axis=1)
    valid_rows = (jnp.arange(BLOCK_LEN, dtype=jnp.int32) < BLOCK_LEN - shift)[None, :, None]
    pair_count = (2 * DRAWS * (BLOCK_LEN - shift)).astype(jnp.float32)
    earlier = jnp.where(valid_rows, features.astype(jnp.float32), 0.0)
    later = jnp.where(valid_rows, shifted.astype(jnp.float32), 0.0)
    feature_mean = (jnp.sum(earlier, axis=(0, 1)) + jnp.sum(later, axis=(0, 1))) / pair_count
    zero_lag = (
        jnp.where(valid_rows, earlier - feature_mean, 0.0).astype(jnp.bfloat16).reshape(-1, width)
    )
    lagged = (
        jnp.where(valid_rows, later - feature_mean, 0.0).astype(jnp.bfloat16).reshape(-1, width)
    )
    return (zero_lag, lagged, pair_count)


def shards(coordinates, resample, block_slot, lag_time, atom_pairs):
    chosen = gather_blocks(coordinates, resample, block_slot)
    width = F // lax.axis_size("row")
    shift = lag_time[0]
    zero_row, lag_row, pair_count = tile_features(
        chosen, atom_pairs, lax.axis_index("row") * width, width, shift
    )
    row_stack = jnp.concatenate([zero_row, lag_row], axis=0)
    zero_col, lag_col, unused_count = tile_features(
        chosen, atom_pairs, lax.axis_index("col") * width, width, shift
    )
    col_stack = jnp.concatenate([zero_col, lag_col], axis=0)
    half_rows = col_stack.shape[0] // 2
    mirrored = jnp.concatenate([col_stack[half_rows:], col_stack[:half_rows]], axis=0)
    instant = (
        jnp.einsum("na,nb->ab", row_stack, col_stack, preferred_element_type=jnp.float32)
        / pair_count
    )
    crossed = (
        jnp.einsum("na,nb->ab", row_stack, mirrored, preferred_element_type=jnp.float32)
        / pair_count
    )
    return (instant[None].astype(jnp.bfloat16), crossed[None].astype(jnp.bfloat16))


def solution(mesh):
    return jax.shard_map(
        shards,
        mesh=mesh,
        in_specs=(P("rep", None, None, None), P("rep", None), P(), P("rep"), P()),
        out_specs=(P("rep", "row", "col"), P("rep", "row", "col")),
        check_vma=False,
    )
```

profile of v0, /device:TPU:2, one launch (start us, length us, event | category | flops | bytes accessed | tf_op | source)
XLA Modules:
  0.0 108.9 jit_solution(13588767077936588273)
XLA Ops:
  0.6 0.0 copy-start
  0.7 0.9 fusion.48
  1.6 0.0 copy-done
  1.6 36.8 %all_gather.6 = bf16[128,2,3,128]{3,1,2,0:T(2,128)(2,1)S(1)} all-gather(bf16[4,2,3,128]{3,1,2,0:T(2,128)(2,1)S(1)} %constant_dynamic-slice_fusion.4), channel_id=1, replica_groups=mesh['rep'=32,'row'=4,'col'=4] {'rep'}, dimensions={0}, use_global_device_ids=true | all-gather | bytes 202752 | tf_op jit(solution)/shard_map/all_gather | solution.py:21
  38.4 0.7 fusion.47
  39.0 1.4 %gather_fusion = s32[22]{0:T(128)S(1)} fusion(s32[128]{0:T(128)} %param.7, s32[1024]{0:T(1024)S(1)} %pad_clamp_fusion.1), kind=kCustom, calls=%fused_computation | custom fusion | bytes 264 | tf_op jit(solution)/shard_map/jit(_take)/gather | solution.py:22
  40.4 0.7 fusion.44
  41.1 0.6 gather_fusion.1
  41.7 0.7 compare_and_fusion
  42.4 0.1 broadcast_select_fusion
  42.5 24.1 %all_gather.7 = bf16[22,32,3,128]{3,0,2,1:T(8,128)(2,1)S(1)} all-gather(bf16[22,2,3,128]{3,0,2,1:T(8,128)(2,1)S(1)} %copy.13), channel_id=1, replica_groups=mesh['rep'=32,'row'=4,'col'=4] {'row','col'}, dimensions={1}, use_global_device_ids=true | all-gather | bytes 574464 | tf_op jit(solution)/shard_map/all_gather | solution.py:26
  66.6 1.3 %fusion.32 = f32[22,32,3,1024]{3,1,0,2:T(8,128)S(1)} fusion(bf16[22,32,3,128]{3,0,2,1:T(8,128)(2,1)S(1)} %all_gather.7, s32[1024]{0:T(1024)S(1)} %bitcast.60, s32[1024]{0:T(1024)S(1)} %bitcast.58), kind=kOutput, calls=%fused_computation.51 | convolution fusion | flops 554434560 | bytes 9199616 | tf_op jit(solution)/shard_map/dot_general | solution.py:38
  68.0 0.0 copy-start.1
  68.0 1.2 %fusion.49 = bf16[22,32,1024]{2,1,0:T(8,128)(2,1)S(1)} fusion(f32[22,32,3,1024]{3,1,0,2:T(8,128)S(1)} %fusion.32), kind=kLoop, calls=%fused_computation.90 | loop fusion | flops 4325376 | bytes 10092544 | tf_op jit(solution)/shard_map/sqrt | solution.py:46
  69.2 2.1 %copy-done.1 = f32[22,32,3,1024]{3,1,0,2:T(8,128)} copy-done((f32[22,32,3,1024]{3,1,0,2:T(8,128)}, f32[22,32,3,1024]{3,1,0,2:T(8,128)S(1)}, u32[]{:S(2)}) %copy-start.1) | copy-done | bytes 8650776
  71.3 1.3 %fusion.34 = f32[22,32,3,1024]{3,1,2,0:T(8,128)S(1)} fusion(bf16[22,32,3,128]{3,0,2,1:T(8,128)(2,1)S(1)} %all_gather.7, s32[1024]{0:T(1024)S(1)} %bitcast.59, s32[1024]{0:T(1024)S(1)} %bitcast.57), kind=kOutput, calls=%fused_computation.53 | convolution fusion | flops 554434560 | bytes 9199616 | tf_op jit(solution)/shard_map/dot_general | solution.py:38
  72.6 0.0 copy-start.2
  72.6 1.2 %fusion.50 = bf16[22,32,1024]{2,1,0:T(8,128)(2,1)S(1)} fusion(f32[22,32,3,1024]{3,1,2,0:T(8,128)S(1)} %fusion.34), kind=kLoop, calls=%fused_computation.91 | loop fusion | flops 4325376 | bytes 10092544 | tf_op jit(solution)/shard_map/sqrt | solution.py:46
  73.9 2.1 %copy-done.2 = f32[22,32,3,1024]{3,1,2,0:T(8,128)} copy-done((f32[22,32,3,1024]{3,1,2,0:T(8,128)}, f32[22,32,3,1024]{3,1,2,0:T(8,128)S(1)}, u32[]{:S(2)}) %copy-start.2) | copy-done | bytes 8650776
  76.6 8.7 %fusion.23 = (f32[1024]{0:T(1024)S(1)}, f32[1024]{0:T(1024)S(1)}, f32[1024]{0:T(1024)S(1)}, f32[1024]{0:T(1024)S(1)}) fusion(pred[32]{0:T(512)(128)(4,1)S(1)} %iota_compare_fusion.4, s32[]{:T(128)S(6)} %select_n.115, bf16[22,32,1024]{2,1,0:T(8,128)(2,1)S(1)} %fusion.50, bf16[22,32,1024]{2,1,0:T(8,128)(2,1)S(1)} %fusion.49, f32[22,32,3,1024]{3,1,0,2:T(8,128)} %copy-done.1, ...), kind=kLoop, calls=%fused_computation.45 | loop fusion | flops 21622784 | bytes 20201508 | tf_op jit(solution)/shard_map/reduce_sum | solution.py:53
  85.4 0.0 copy-start.3
  85.4 6.0 %fusion.2 = bf16[22,32,1,1024]{3,1,0,2:T(8,128)(2,1)} fusion(f32[22,32,3,1024]{3,1,0,2:T(8,128)} %copy-done.1), kind=kLoop, calls=%fused_computation.7 | loop fusion | flops 4325376 | bytes 10092544 | tf_op jit(solution)/shard_map/convert.1
  91.4 0.1 copy-done.3
  91.5 2.3 %fusion.6 = bf16[22,32,1,1024]{3,1,2,0:T(8,128)(2,1)} fusion(f32[22,32,3,1024]{3,1,2,0:T(8,128)S(1)} %copy-done.3), kind=kLoop, calls=%fused_computation.14 | loop fusion | flops 4325376 | bytes 10092544 | tf_op jit(solution)/shard_map/convert.3
  93.8 0.1 broadcast_in_dim.75
  93.9 3.1 %fusion.21 = (bf16[704,1024]{1,0:T(8,128)(2,1)S(1)}, bf16[704,1024]{1,0:T(8,128)(2,1)S(1)}) fusion(bf16[22,32,1,1024]{3,1,2,0:T(8,128)(2,1)} %fusion.6, f32[1024]{0:T(1024)S(1)} %get-tuple-element.17, pred[704]{0:T(1024)(128)(4,1)S(1)} %broadcast_in_dim.75, f32[1024]{0:T(1024)S(1)} %get-tuple-element.16, bf16[22,32,1,1024]{3,1,0,2:T(8,128)(2,1)} %fusion.2), kind=kLoop, calls=%fused_computation.38 | loop fusion | flops 7208960 | bytes 5776064 | tf_op jit(solution)/shard_map/convert_element_type | solution.py:55
  97.0 2.6 %select_convert_fusion.1 = (bf16[22,32,1024]{2,1,0:T(8,128)(2,1)S(1)}, bf16[22,32,1024]{2,1,0:T(8,128)(2,1)S(1)}) fusion(f32[1024]{0:T(1024)S(1)} %get-tuple-element.17, pred[32]{0:T(512)(128)(4,1)S(1)} %iota_compare_fusion.4, s32[]{:T(128)S(6)} %select_n.115, bf16[22,32,1024]{2,1,0:T(8,128)(2,1)S(1)} %fusion.50, f32[1024]{0:T(1024)S(1)} %get-tuple-element.16, ...), kind=kLoop, calls=%fused_computation.43 | loop fusion | flops 11534336 | bytes 5775396 | tf_op jit(solution)/shard_map/convert_element_type | solution.py:58
  99.6 4.7 %fusion.25 = bf16[1,1024,1024]{2,1,0:T(8,128)(2,1)} fusion(f32[]{:T(128)S(6)} %convert_element_type.76, bf16[704,1024]{1,0:T(8,128)(2,1)S(1)} %get-tuple-element.13, bf16[704,1024]{1,0:T(8,128)(2,1)S(1)} %bitcast.55, bf16[704,1024]{1,0:T(8,128)(2,1)S(1)} %bitcast.53, bf16[704,1024]{1,0:T(8,128)(2,1)S(1)} %get-tuple-element.12), kind=kOutput, calls=%fused_computation.48 | convolution fusion | flops 2966421504 | bytes 7864324 | tf_op jit(solution)/shard_map/na,nb->ab/dot_general | solution.py:82
  104.3 4.6 %fusion.24 = bf16[1,1024,1024]{2,1,0:T(8,128)(2,1)} fusion(f32[]{:T(128)S(6)} %convert_element_type.76, bf16[704,1024]{1,0:T(8,128)(2,1)S(1)} %bitcast.56, bf16[704,1024]{1,0:T(8,128)(2,1)S(1)} %get-tuple-element.13, bf16[704,1024]{1,0:T(8,128)(2,1)S(1)} %bitcast.54, bf16[704,1024]{1,0:T(8,128)(2,1)S(1)} %get-tuple-element.12), kind=kOutput, calls=%fused_computation.47 | convolution fusion | flops 2966421504 | bytes 7864324 | tf_op jit(solution)/shard_map/na,nb->ab/dot_general | solution.py:78
  (9 shorter events, 0.1 us)
Async XLA Ops:
  0.6 0.9 copy-start
  68.0 3.3 %copy-start.1 = (f32[22,32,3,1024]{3,1,0,2:T(8,128)}, f32[22,32,3,1024]{3,1,0,2:T(8,128)S(1)}, u32[]{:S(2)}) copy-start(f32[22,32,3,1024]{3,1,0,2:T(8,128)S(1)} %fusion.32) | copy-start | bytes 25952260
  72.6 3.3 %copy-start.2 = (f32[22,32,3,1024]{3,1,2,0:T(8,128)}, f32[22,32,3,1024]{3,1,2,0:T(8,128)S(1)}, u32[]{:S(2)}) copy-start(f32[22,32,3,1024]{3,1,2,0:T(8,128)S(1)} %fusion.34) | copy-start | bytes 25952260
  85.4 6.1 %copy-start.3 = (f32[22,32,3,1024]{3,1,2,0:T(8,128)S(1)}, f32[22,32,3,1024]{3,1,2,0:T(8,128)}, u32[]{:S(2)}) copy-start(f32[22,32,3,1024]{3,1,2,0:T(8,128)} %copy-done.2) | copy-start | bytes 25952260
where the time goes:
time: 109 us
  blocking collectives  60.9 us (56%)
  other arithmetic  27.3 us (25%)
  matrix products  11.9 us (11%)
  local copies, waits for them, and re-layouts  7.29 us (7%)
  between operations  1.46 us (1%)
    all_gather x1, blocking collectives, gather_blocks(): every = lax.all_gather(piece, 'rep', axis=0, tiled=True)  36.8 us
    all_gather x1, blocking collectives, gather_blocks(): return lax.all_gather(picked, ('row', 'col'), axis=1, tiled=True)  24.1 us
    reduce_sum x1, other arithmetic, tile_features(): jnp.sum(later, axis=(0, 1))  8.72 us
    another operation x2, other arithmetic  8.31 us
    dot_general x1, matrix products, shards(): jnp.einsum('na,nb->ab', row_stack, mirrored, preferred_element_type=jnp.f...  4.67 us
    dot_general x1, matrix products, shards(): jnp.einsum('na,nb->ab', row_stack, col_stack, preferred_element_type=jnp....  4.64 us
    unnamed x8, local copies, waits for them, and re-layouts  4.3 us
    convert_element_type x1, other arithmetic, tile_features(): jnp.where(valid_rows, earlier - feature_mean, 0.0).astype(jnp.bfloat16)  3.09 us

commit v1 on v0

--- a/solution.py
+++ b/solution.py
@@ -7,6 +7,12 @@
 ATOMS = 128
 BLOCK_LEN = 32
 DRAWS = 22
+produce_state_on_mesh = lambda inner_x, bus_axis, out_dim: jnp.concatenate(
+    lax.all_to_all(
+        jnp.stack([inner_x for _ in range(lax.axis_size(bus_axis))], axis=0), bus_axis, 0, 0
+    ),
+    axis=out_dim,
+)
 
 
 def gather_blocks(coordinates, resample, block_slot):
@@ -23,7 +29,7 @@
     picked = jnp.take(every, slots, axis=0)
     if groups == 1:
         return picked
-    return lax.all_gather(picked, ("row", "col"), axis=1, tiled=True)
+    return produce_state_on_mesh(picked, ("row", "col"), out_dim=1)
 
 
 def tile_features(chosen, atom_pairs, first_feature, width, shift):

time: 109 us -> 87.9 us (0.81)
  the two profiles are of different devices: /device:TPU:2 before, /device:TPU:1 now
where the time goes in v1:
time: 87.9 us; the launch traced here: 87.5 us
  blocking collectives  38.1 us (43%)
  other arithmetic  16.2 us (18%)
  matrix products  11.9 us (14%)
  waiting for transfers between devices  8.68 us (10%)
  starting transfers between devices  6.75 us (8%)
  local copies, waits for them, and re-layouts  4.42 us (5%)
  between operations  1.42 us (2%)
    all_gather x1, blocking collectives, gather_blocks(): every = lax.all_gather(piece, 'rep', axis=0, tiled=True)  38.1 us
    all_to_all x1, waiting for transfers between devices, lax.all_to_all(jnp.stack([inner_x for _ in range(lax.axis_size(bus_axis))...  8.68 us
    all_to_all x1, starting transfers between devices, lax.all_to_all(jnp.stack([inner_x for _ in range(lax.axis_size(bus_axis))...  6.75 us
    reduce_sum x1, other arithmetic, tile_features(): jnp.sum(later, axis=(0, 1))  5.25 us
    dot_general x1, matrix products, shards(): jnp.einsum('na,nb->ab', row_stack, mirrored, preferred_element_type=jnp.f...  4.66 us
    dot_general x1, matrix products, shards(): jnp.einsum('na,nb->ab', row_stack, col_stack, preferred_element_type=jnp....  4.65 us
    convert_element_type x1, other arithmetic, tile_features(): jnp.where(valid_rows, later - feature_mean, 0.0).astype(jnp.bfloat16)  2.62 us
    dot_general x2, matrix products, tile_features(): jnp.dot(flat, signed, preferred_element_type=jnp.float32)  2.61 us
  transfers between devices with their start and end apart: 1, of which 1 were waited for; matrix products, arithmetic and copies ran while one was open for 1% of the time, Pallas kernels for 0%

profile of v1, /device:TPU:1, one launch (start us, length us, event | category | flops | bytes accessed | tf_op | source)
XLA Modules:
  0.0 87.5 jit_solution(13975090137176518192)
XLA Ops:
  0.6 0.0 copy-start
  0.6 0.7 fusion.46
  1.3 1.4 %gather_fusion = s32[22]{0:T(128)S(1)} fusion(s32[128]{0:T(128)} %param.7, s32[1024]{0:T(1024)S(1)} %pad_clamp_fusion.1), kind=kCustom, calls=%fused_computation | custom fusion | bytes 264 | tf_op jit(solution)/shard_map/jit(_take)/gather | solution.py:28
  2.7 0.7 fusion.43
  3.4 0.7 compare_and_fusion
  4.0 0.0 copy-done
  4.1 38.1 %all_gather.3 = bf16[128,2,3,128]{3,1,2,0:T(2,128)(2,1)S(1)} all-gather(bf16[4,2,3,128]{3,1,2,0:T(2,128)(2,1)S(1)} %constant_dynamic-slice_fusion.4), channel_id=1, replica_groups=mesh['rep'=32,'row'=4,'col'=4] {'rep'}, dimensions={0}, use_global_device_ids=true | all-gather | bytes 202752 | tf_op jit(solution)/shard_map/all_gather | solution.py:27
  42.2 0.6 gather_fusion.1
  42.8 0.1 broadcast_select_fusion
  42.9 1.1 %stack.2 = bf16[16,22,2,3,128]{4,2,3,1,0:T(2,128)(2,1)} broadcast(bf16[22,2,3,128]{3,1,2,0:T(2,128)(2,1)S(1)} %broadcast_select_fusion), dimensions={1,2,3,4} | broadcast | bytes 574464 | tf_op jit(solution)/shard_map/stack | solution.py:12
  44.0 6.8 %all-to-all-start = ((bf16[16,22,2,3,128]{4,2,3,1,0:T(2,128)(2,1)}), bf16[16,22,2,3,128]{4,2,3,1,0:T(2,128)(2,1)S(1)}, u32[]{:S(2)}, u32[]{:S(2)}) async-start(bf16[16,22,2,3,128]{4,2,3,1,0:T(2,128)(2,1)} %stack.2), calls=%async_computation | async-start | bytes 1081344 | tf_op jit(solution)/shard_map/all_to_all | solution.py:11
  50.8 0.9 fusion.47
  52.3 0.1 broadcast_in_dim.75
  52.4 8.7 %all-to-all-done = bf16[16,22,2,3,128]{4,2,3,1,0:T(2,128)(2,1)S(1)} async-done(((bf16[16,22,2,3,128]{4,2,3,1,0:T(2,128)(2,1)}), bf16[16,22,2,3,128]{4,2,3,1,0:T(2,128)(2,1)S(1)}, u32[]{:S(2)}, u32[]{:S(2)}) %all-to-all-start) | async-done | bytes 540704 | tf_op jit(solution)/shard_map/all_to_all | solution.py:11
  61.1 0.4 copy.13
  61.5 1.3 %fusion.32 = f32[22,32,3,1024]{3,1,0,2:T(8,128)S(1)} fusion(bf16[22,32,3,128]{3,1,2,0:T(8,128)(2,1)S(1)} %bitcast.56, s32[1024]{0:T(1024)S(1)} %bitcast.66, s32[1024]{0:T(1024)S(1)} %bitcast.65), kind=kOutput, calls=%fused_computation.51 | convolution fusion | flops 554434560 | bytes 9199616 | tf_op jit(solution)/shard_map/dot_general | solution.py:44
  62.8 1.2 %fusion.49 = bf16[22,32,1024]{2,1,0:T(8,128)(2,1)S(1)} fusion(f32[22,32,3,1024]{3,1,0,2:T(8,128)S(1)} %fusion.32), kind=kLoop, calls=%fused_computation.89 | loop fusion | flops 4325376 | bytes 10092544 | tf_op jit(solution)/shard_map/sqrt | solution.py:52
  64.0 1.2 %fusion.2 = bf16[22,32,1,1024]{3,1,0,2:T(8,128)(2,1)S(1)} fusion(f32[22,32,3,1024]{3,1,0,2:T(8,128)S(1)} %fusion.32), kind=kLoop, calls=%fused_computation.7 | loop fusion | flops 4325376 | bytes 10092544 | tf_op jit(solution)/shard_map/convert.1
  65.2 1.3 %fusion.35 = f32[22,32,3,1024]{3,1,2,0:T(8,128)S(1)} fusion(bf16[22,32,3,128]{3,1,2,0:T(8,128)(2,1)S(1)} %bitcast.57, s32[1024]{0:T(1024)S(1)} %bitcast.64, s32[1024]{0:T(1024)S(1)} %bitcast.63), kind=kOutput, calls=%fused_computation.60 | convolution fusion | flops 554434560 | bytes 9199616 | tf_op jit(solution)/shard_map/dot_general | solution.py:44
  66.5 1.2 %fusion.50 = bf16[22,32,1024]{2,1,0:T(8,128)(2,1)S(1)} fusion(f32[22,32,3,1024]{3,1,2,0:T(8,128)S(1)} %fusion.35), kind=kLoop, calls=%fused_computation.90 | loop fusion | flops 4325376 | bytes 10092544 | tf_op jit(solution)/shard_map/sqrt | solution.py:52
  67.7 1.2 %fusion.6 = bf16[22,32,1,1024]{3,1,2,0:T(8,128)(2,1)S(1)} fusion(f32[22,32,3,1024]{3,1,2,0:T(8,128)S(1)} %fusion.35), kind=kLoop, calls=%fused_computation.14 | loop fusion | flops 4325376 | bytes 10092544 | tf_op jit(solution)/shard_map/convert.3
  68.9 5.2 %fusion.23 = (f32[1024]{0:T(1024)S(1)}, f32[1024]{0:T(1024)S(1)}, f32[1024]{0:T(1024)S(1)}, f32[1024]{0:T(1024)S(1)}) fusion(pred[32]{0:T(512)(128)(4,1)S(1)} %iota_compare_fusion.4, s32[]{:T(128)S(6)} %select_n.117, bf16[22,32,1024]{2,1,0:T(8,128)(2,1)S(1)} %fusion.50, bf16[22,32,1024]{2,1,0:T(8,128)(2,1)S(1)} %fusion.49, ...), kind=kLoop, calls=%fused_computation.45 | loop fusion | flops 21622784 | bytes 20201508 | tf_op jit(solution)/shard_map/reduce_sum | solution.py:59
  74.2 2.6 %select_convert_fusion.1 = (bf16[22,32,1024]{2,1,0:T(8,128)(2,1)S(1)}, bf16[22,32,1024]{2,1,0:T(8,128)(2,1)S(1)}) fusion(f32[1024]{0:T(1024)S(1)} %get-tuple-element.17, pred[32]{0:T(512)(128)(4,1)S(1)} %iota_compare_fusion.4, s32[]{:T(128)S(6)} %select_n.117, bf16[22,32,1024]{2,1,0:T(8,128)(2,1)S(1)} %fusion.50, f32[1024]{0:T(1024)S(1)} %get-tuple-element.16, ...), kind=kLoop, calls=%fused_computation.43 | loop fusion | flops 11534336 | bytes 5775396 | tf_op jit(solution)/shard_map/convert_element_type | solution.py:64
  76.8 1.4 %fusion.21 = (bf16[704,1024]{1,0:T(8,128)(2,1)S(1)}, bf16[704,1024]{1,0:T(8,128)(2,1)S(1)}) fusion(bf16[22,32,1,1024]{3,1,2,0:T(8,128)(2,1)S(1)} %fusion.6, f32[1024]{0:T(1024)S(1)} %get-tuple-element.17, pred[704]{0:T(1024)(128)(4,1)S(1)} %broadcast_in_dim.75, f32[1024]{0:T(1024)S(1)} %get-tuple-element.16, bf16[22,32,1,1024]{3,1,0,2:T(8,128)(2,1)S(1)} %fusion.2), kind=kLoop, calls=%fused_computation.38 | loop fusion | flops 7208960 | bytes 5776064 | tf_op jit(solution)/shard_map/convert_element_type | solution.py:61
  78.2 4.7 %fusion.25 = bf16[1,1024,1024]{2,1,0:T(8,128)(2,1)} fusion(f32[]{:T(128)S(6)} %convert_element_type.76, bf16[704,1024]{1,0:T(8,128)(2,1)S(1)} %get-tuple-element.13, bf16[704,1024]{1,0:T(8,128)(2,1)S(1)} %bitcast.61, bf16[704,1024]{1,0:T(8,128)(2,1)S(1)} %bitcast.59, bf16[704,1024]{1,0:T(8,128)(2,1)S(1)} %get-tuple-element.12), kind=kOutput, calls=%fused_computation.48 | convolution fusion | flops 2966421504 | bytes 7864324 | tf_op jit(solution)/shard_map/na,nb->ab/dot_general | solution.py:88
  82.9 4.6 %fusion.24 = bf16[1,1024,1024]{2,1,0:T(8,128)(2,1)} fusion(f32[]{:T(128)S(6)} %convert_element_type.76, bf16[704,1024]{1,0:T(8,128)(2,1)S(1)} %bitcast.62, bf16[704,1024]{1,0:T(8,128)(2,1)S(1)} %get-tuple-element.13, bf16[704,1024]{1,0:T(8,128)(2,1)S(1)} %bitcast.60, bf16[704,1024]{1,0:T(8,128)(2,1)S(1)} %get-tuple-element.12), kind=kOutput, calls=%fused_computation.47 | convolution fusion | flops 2966421504 | bytes 7864324 | tf_op jit(solution)/shard_map/na,nb->ab/dot_general | solution.py:84
  (8 shorter events, 0.1 us)
Async XLA Ops:
  0.6 3.4 %copy-start = (bf16[4,32,3,128]{3,1,2,0:T(8,128)(2,1)S(1)}, bf16[4,32,3,128]{3,1,2,0:T(8,128)(2,1)}, u32[]{:S(2)}) copy-start(bf16[4,32,3,128]{3,1,2,0:T(8,128)(2,1)} %param.5) | copy-start | bytes 294916
  44.0 17.1 %all-to-all-start = ((bf16[16,22,2,3,128]{4,2,3,1,0:T(2,128)(2,1)}), bf16[16,22,2,3,128]{4,2,3,1,0:T(2,128)(2,1)S(1)}, u32[]{:S(2)}, u32[]{:S(2)}) async-start(bf16[16,22,2,3,128]{4,2,3,1,0:T(2,128)(2,1)} %stack.2), calls=%async_computation | async-start | bytes 1081344 | tf_op jit(solution)/shard_map/all_to_all | solution.py:11
